TPU v7x, 256 devices: a whole 4x4x8 slice. The times are simulated.
256 devices in a mesh: sec: 16 (over x, y), vel: 16 (over z, core).
Axes of the slice: x: 4, y: 4, z: 8, core: 2. Of those that a mesh axis runs over, the one named last changes fastest.
Arguments:
- distribution: float32 [13824, 4096], P('vel', 'sec'), may hold values from -6 to 6
- collision: float32 [4096], P('sec'), may hold values from 0.05 to 2
- lower_blocks: float32 [25, 4096], P(None, 'sec'), may hold values from -0.6 to 0.6
- upper_blocks: float32 [25, 4096], P(None, 'sec'), may hold values from -0.6 to 0.6
- diag_inverse: float32 [25, 4096], P(None, 'sec'), may hold values from -0.2 to 1.4
Outputs:
- new_distribution: float32 [13824, 4096], P('vel', 'sec')
- macro: float32 [5, 4096], P(None, 'sec')
All inputs are finite; a program needn't handle non-finite values.
Results may differ from a plain program's by a relative error of at most 0.0003.
Values sent between devices are 32-bit elements; how exact they have to be, the bound alone decides.
No kernel may reach another device: no remote copies, remote signals or barrier semaphores. Data moves between devices by JAX's collectives and lax.ppermute only.
A program may use at most 64 MiB of HBM per device.

v0:
```python
import math
import jax
import jax.numpy as jnp
import numpy as np
from jax import lax
from jax.sharding import PartitionSpec as P

NXI = 24
TUBES = 128
JACOBI = 4
NEWTON = 2
HIGH = lax.Precision.HIGHEST
pseudo_rate = 1.0


def passed_along(block, axis, distance):
    devices = range(lax.axis_size(axis))
    route = [(i - distance, i) for i in devices if i - distance in devices]
    return lax.ppermute(block, axis, route)


def extended(array, sides, width):
    for axis, dim in sides:
        count, length = (lax.axis_size(axis), array.shape[dim])
        up = [(i, (i + 1) % count) for i in range(count - 1)]
        down = [(j, i) for i, j in up]
        last = lax.slice_in_dim(array, length - width, length, axis=dim)
        first = lax.slice_in_dim(array, 0, width, axis=dim)
        before = lax.ppermute(last, axis, up)
        after = lax.ppermute(first, axis, down)
        array = jnp.concatenate([before, array, after], axis=dim)
    return array


def hermite_rule(count):
    quarter = math.pi ** (-0.25)
    found = []
    last_slope = 1.0
    for index in range(count // 2):
        if index == 0:
            guess = math.sqrt(2.0 * count + 1.0) - 1.85575 * (2.0 * count + 1.0) ** (-0.16667)
        elif index == 1:
            guess = guess - 1.14 * count**0.426 / guess
        elif index == 2:
            guess = 1.86 * guess - 0.86 * found[0][0]
        elif index == 3:
            guess = 1.91 * guess - 0.91 * found[1][0]
        else:
            guess = 2.0 * guess - found[index - 2][0]
        for repeat in range(60):
            current = quarter
            previous = 0.0
            for order in range(count):
                older = previous
                previous = current
                current = (
                    guess * math.sqrt(2.0 / (order + 1)) * previous
                    - math.sqrt(order / (order + 1.0)) * older
                )
            last_slope = math.sqrt(2.0 * count) * previous
            guess = guess - current / last_slope
        found.append((guess, 2.0 / (last_slope * last_slope)))
    positive = found[::-1]
    points = [-pair[0] for pair in found] + [pair[0] for pair in positive]
    weights = [pair[1] for pair in found] + [pair[1] for pair in positive]
    return (np.array(points), np.array(weights))


def node_tables(axis_points):
    points, weights = hermite_rule(axis_points)
    node_index = np.arange(axis_points**3)
    idx_x = node_index % axis_points
    idx_z = node_index // axis_points % axis_points
    idx_y = node_index // (axis_points * axis_points)
    along_x = points[idx_x]
    along_y = points[idx_y]
    along_z = points[idx_z]
    node_weight = weights[idx_x] * weights[idx_y] * weights[idx_z] / math.pi**1.5
    energy = along_x**2 + along_y**2 + along_z**2 - 1.5
    moment_basis = np.stack([along_x * 0.0 + 1.0, along_x, along_y, along_z, energy])
    norm_scale = np.array([1.0, 0.5, 0.5, 0.5, 1.5])
    return (
        along_x,
        node_weight,
        moment_basis * node_weight[None, :],
        moment_basis / norm_scale[:, None],
    )


def apply_block(matrices, vector):
    shaped = matrices.reshape((5, 5) + vector.shape[1:])
    return jnp.sum(shaped * vector[None], axis=1)


def affine_combine(earlier_map, later_map):
    return (later_map[0] * earlier_map[0], later_map[0] * earlier_map[1] + later_map[1])


def newton_sums(loaded, signed, shift_mass, shift_flow):
    growth = jnp.exp(shift_mass + shift_flow * signed)
    scaled = loaded * growth
    excess = loaded * (growth - 1.0)
    return jnp.stack(
        [
            jnp.sum(scaled),
            jnp.sum(scaled * signed),
            jnp.sum(scaled * signed * signed),
            jnp.sum(excess),
            jnp.sum(excess * signed),
        ]
    )


def newton_update(shift_mass, shift_flow, sums, goal_mass, goal_flow):
    resid_mass = sums[3] - goal_mass
    resid_flow = sums[4] - goal_flow
    determinant = sums[0] * sums[2] - sums[1] * sums[1]
    new_mass = shift_mass - (sums[2] * resid_mass - sums[1] * resid_flow) / determinant
    new_flow = shift_flow - (sums[0] * resid_flow - sums[1] * resid_mass) / determinant
    return (new_mass, new_flow)


def received(block, distance):
    count = lax.axis_size("sec")
    if abs(distance) >= count:
        return jnp.zeros_like(block)
    return passed_along(block, "sec", distance)


def exclusive_inflow(rate, drive, sign):
    count = lax.axis_size("sec")

    def fetch(a, b, distance):
        got = received(jnp.concatenate([a, b], axis=0), sign * distance)
        return (got[:1], got[1:])

    near_a, near_b = fetch(rate, drive, 1)
    span = 1
    if count > 2:
        far_a, far_b = fetch(rate, drive, 2)
        near_a, near_b = (near_a * far_a, near_a * far_b + near_b)
        span = 2
    while span < count - 1:
        got_a, got_b = fetch(near_a, near_b, span)
        near_a, near_b = (near_a * got_a, near_a * got_b + near_b)
        span *= 2
    return near_b


def with_halo(array, width):
    parts = [received(array, d) for d in range(width, 0, -1)]
    parts.append(array)
    parts.extend((received(array, -d) for d in range(1, width + 1)))
    return jnp.concatenate(parts, axis=1)


def body(distribution, collision, lower_blocks, upper_blocks, diag_inverse):
    node_count = distribution.shape[0]
    cell_count = distribution.shape[1]
    length = cell_count // TUBES
    node_rows = node_count // NXI
    half_nodes = NXI // 2
    along_x, node_weight, weighted_np, rebuild_np = node_tables(NXI)
    all_mass = jnp.asarray(node_weight, jnp.float32)
    offset = lax.axis_index("vel") * node_count
    weighted = lax.dynamic_slice_in_dim(
        jnp.asarray(weighted_np, jnp.float32), offset, node_count, 1
    )
    rebuild = lax.dynamic_slice_in_dim(jnp.asarray(rebuild_np, jnp.float32), offset, node_count, 1)
    node_mass = lax.dynamic_slice_in_dim(all_mass, offset, node_count, 0)
    line_signed = jnp.asarray(along_x[:NXI], jnp.float32)
    old_moments = lax.psum(jnp.dot(weighted, distribution, precision=HIGH), "vel")
    target = jnp.dot(rebuild.T, old_moments, precision=HIGH)
    total_length = length * lax.axis_size("sec")
    thickness = collision.reshape(1, 1, length, TUBES)
    node_speed = jnp.abs(line_signed).reshape(1, NXI, 1, 1)
    denominator = node_speed * total_length + thickness + pseudo_rate
    carry_rate = node_speed * total_length / denominator
    drive_term = (
        thickness * target.reshape(node_rows, NXI, length, TUBES)
        + pseudo_rate * distribution.reshape(node_rows, NXI, length, TUBES)
    ) / denominator
    prod_neg, local_neg = lax.associative_scan(
        affine_combine,
        (
            jnp.broadcast_to(carry_rate[:, :half_nodes], (1, half_nodes, length, TUBES)),
            drive_term[:, :half_nodes],
        ),
        reverse=True,
        axis=2,
    )
    prod_pos, local_pos = lax.associative_scan(
        affine_combine,
        (
            jnp.broadcast_to(carry_rate[:, half_nodes:], (1, NXI - half_nodes, length, TUBES)),
            drive_term[:, half_nodes:],
        ),
        axis=2,
    )
    inflow_pos = exclusive_inflow(prod_pos[:, :, -1], local_pos[:, :, -1], 1)
    inflow_neg = exclusive_inflow(prod_neg[:, :, 0], local_neg[:, :, 0], -1)
    field_neg = local_neg + prod_neg * inflow_neg[:, :, None, :]
    field_pos = local_pos + prod_pos * inflow_pos[:, :, None, :]
    half_field = jnp.concatenate([field_neg, field_pos], axis=1).reshape(node_count, cell_count)
    half_moments = lax.psum(jnp.dot(weighted, half_field, precision=HIGH), "vel")
    residual = (half_moments - old_moments).reshape(5, length, TUBES)
    width = min(-(-JACOBI // length), lax.axis_size("sec") - 1)
    blocks = jnp.concatenate([lower_blocks, upper_blocks, diag_inverse], axis=0)
    blocks_wide = with_halo(blocks.reshape(75, length, TUBES), width)
    lower_r = blocks_wide[:25]
    upper_r = blocks_wide[25:50]
    inverse_r = blocks_wide[50:]
    residual_wide = with_halo(residual, width)
    correction = apply_block(inverse_r, residual_wide)
    edge_zero = jnp.zeros((5, 1, TUBES), jnp.float32)
    for sweep_index in range(JACOBI):
        from_left = jnp.concatenate([edge_zero, correction[:, :-1]], axis=1)
        from_right = jnp.concatenate([correction[:, 1:], edge_zero], axis=1)
        correction = apply_block(
            inverse_r,
            residual_wide - apply_block(lower_r, from_left) - apply_block(upper_r, from_right),
        )
    correction = correction[:, width * length : (width + 1) * length].reshape(5, cell_count)
    macro = half_moments + correction
    synthetic = half_field + jnp.dot(rebuild.T, correction, precision=HIGH)
    local_totals = jnp.sum(old_moments - macro, axis=1)[0:2]
    magnitude = jnp.sum(jnp.abs(synthetic), axis=1)
    line_loaded = jnp.sum((node_mass * magnitude).reshape(node_rows, NXI), axis=0)
    first_copy = (lax.axis_index("vel") == 0).astype(jnp.float32)
    gathered = lax.psum(jnp.concatenate([line_loaded, local_totals * first_copy]), ("sec", "vel"))
    loaded = gathered[:NXI]
    goals = gathered[NXI:]
    shift_mass = jnp.zeros((), jnp.float32)
    shift_flow = jnp.zeros((), jnp.float32)
    for newton_turn in range(NEWTON):
        sums = newton_sums(loaded, line_signed, shift_mass, shift_flow)
        shift_mass, shift_flow = newton_update(shift_mass, shift_flow, sums, goals[0], goals[1])
    growth = jnp.exp(shift_mass + shift_flow * line_signed)
    synthetic_rows = synthetic.reshape(node_rows, NXI, cell_count)
    new_distribution = synthetic_rows + jnp.abs(synthetic_rows) * (growth[None, :, None] - 1.0)
    return (new_distribution.reshape(node_count, cell_count), macro)


def solution(mesh):
    in_specs = (P("vel", "sec"), P("sec"), P(None, "sec"), P(None, "sec"), P(None, "sec"))
    out_specs = (P("vel", "sec"), P(None, "sec"))
    return jax.shard_map(body, mesh=mesh, in_specs=in_specs, out_specs=out_specs, check_vma=False)
```

profile of v0, /device:TPU:1, one launch (start us, length us, event | category | flops | bytes accessed | tf_op | source)
XLA Modules:
  0.0 254.2 jit_solution(769121284347335400)
XLA Ops:
  0.6 0.0 copy-start.6
  0.7 0.7 copy-done.4
  1.3 0.1 add_add_fusion
  1.4 0.1 add_divide_fusion.1
  1.5 0.0 copy-start
  1.5 1.7 reshape.255
  3.2 1.3 fusion.13
  4.5 27.9 %psum.21 = f32[5,256]{1,0:T(8,128)S(1)} all-reduce(f32[5,256]{1,0:T(8,128)S(1)} %fusion.13), channel_id=1, replica_groups=mesh['sec'=16,'vel'=16] {'vel'}, use_global_device_ids=true, to_apply=%region_0.0 | all-reduce | flops 1280 | bytes 10240 | tf_op jit(solution)/shard_map/psum | solution.py:172
  32.4 1.8 fusion.16
  34.3 0.5 reshape.254
  34.8 0.1 add_divide_fusion
  34.9 0.7 fusion.29
  35.6 0.4 fusion.10
  36.0 0.0 copy-start.1
  36.0 0.0 copy-start.2
  36.0 1.3 collective-permute-start
  37.4 1.3 collective-permute-start.1
  38.8 6.2 %collective-permute-start.10 = (f32[75,2,128]{2,1,0:T(2,128)S(1)}, f32[75,2,128]{2,1,0:T(2,128)S(1)}, u32[]{:S(2)}, u32[]{:S(2)}) collective-permute-start(f32[75,2,128]{2,1,0:T(2,128)S(1)} %reshape.257), channel_id=1, source_target_pairs={{0,32},{16,48},{32,64},{48,80},{64,96},{80,112},{96,128},{112,144}... | collective-permute-start | bytes 230408 | tf_op jit(solution)/shard_map/ppermute | solution.py:19
  45.0 3.2 %collective-permute-start.11 = (f32[75,2,128]{2,1,0:T(2,128)S(1)}, f32[75,2,128]{2,1,0:T(2,128)S(1)}, u32[]{:S(2)}, u32[]{:S(2)}) collective-permute-start(f32[75,2,128]{2,1,0:T(2,128)S(1)} %reshape.257), channel_id=1, source_target_pairs={{0,16},{16,32},{32,48},{48,64},{64,80},{80,96},{96,112},{112,128},... | collective-permute-start | bytes 230408 | tf_op jit(solution)/shard_map/ppermute | solution.py:19
  48.3 1.3 collective-permute-start.12
  49.6 0.3 pad_add_fusion.1
  49.9 1.1 rev.8
  51.1 0.4 fusion.11
  51.6 1.3 collective-permute-start.13
  52.9 4.7 %collective-permute-start.5 = (f32[37,12,128]{2,0,1:T(8,128)S(1)}, f32[37,12,128]{2,0,1:T(8,128)S(1)}, u32[]{:S(2)}, u32[]{:S(2)}) collective-permute-start(f32[37,12,128]{2,0,1:T(8,128)S(1)} %pad_maximum_fusion.5), channel_id=1, source_target_pairs={{0,16},{16,32},{32,48},{48,64},{64,80},{80,96},{96,112},{112,128},... | collective-permute-start | bytes 681992 | tf_op jit(solution)/shard_map/ppermute | solution.py:19
  57.6 6.8 %collective-permute-start.6 = (f32[37,12,128]{2,0,1:T(8,128)S(1)}, f32[37,12,128]{2,0,1:T(8,128)S(1)}, u32[]{:S(2)}, u32[]{:S(2)}) collective-permute-start(f32[37,12,128]{2,0,1:T(8,128)S(1)} %pad_maximum_fusion.5), channel_id=1, source_target_pairs={{0,32},{16,48},{32,64},{48,80},{64,96},{80,112},{96,128},{112,144}... | collective-permute-start | bytes 681992 | tf_op jit(solution)/shard_map/ppermute | solution.py:19
  64.4 2.1 concatenate.91
  66.6 0.1 slice_add_fusion.1
  66.7 1.3 collective-permute-start.2
  68.0 0.7 collective-permute-done.6
  68.7 0.1 slice_add_fusion
  68.8 5.4 %collective-permute-start.7 = (f32[37,12,128]{2,0,1:T(8,128)S(1)}, f32[37,12,128]{2,0,1:T(8,128)S(1)}, u32[]{:S(2)}, u32[]{:S(2)}) collective-permute-start(f32[37,12,128]{2,0,1:T(8,128)S(1)} %pad_maximum_fusion.6), channel_id=1, source_target_pairs={{0,32},{16,48},{32,64},{48,80},{64,96},{80,112},{96,128},{112,144}... | collective-permute-start | bytes 681992 | tf_op jit(solution)/shard_map/ppermute | solution.py:19
  74.3 1.2 collective-permute-done.2
  75.5 1.3 collective-permute-start.3
  76.8 4.3 %collective-permute-done.7 = f32[37,12,128]{2,0,1:T(8,128)S(1)} collective-permute-done((f32[37,12,128]{2,0,1:T(8,128)S(1)}, f32[37,12,128]{2,0,1:T(8,128)S(1)}, u32[]{:S(2)}, u32[]{:S(2)}) %collective-permute-start.7) | collective-permute-done | bytes 227360 | tf_op jit(solution)/shard_map/ppermute | solution.py:19
  81.3 8.1 %collective-permute-start.8 = (f32[37,12,128]{2,0,1:T(8,128)S(1)}, f32[37,12,128]{2,0,1:T(8,128)S(1)}, u32[]{:S(2)}, u32[]{:S(2)}) collective-permute-start(f32[37,12,128]{2,0,1:T(8,128)S(1)} %pad_maximum_fusion.7), channel_id=1, source_target_pairs={{0,64},{16,80},{32,96},{48,112},{64,128},{80,144},{96,160},{112,17... | collective-permute-start | bytes 681992 | tf_op jit(solution)/shard_map/ppermute | solution.py:19
  89.4 1.5 collective-permute-done.3
  91.0 1.3 collective-permute-start.4
  92.3 0.2 collective-permute-done.8
  92.6 5.9 %collective-permute-start.9 = (f32[37,12,128]{2,0,1:T(8,128)S(1)}, f32[37,12,128]{2,0,1:T(8,128)S(1)}, u32[]{:S(2)}, u32[]{:S(2)}) collective-permute-start(f32[37,12,128]{2,0,1:T(8,128)S(1)} %pad_maximum_fusion.8), channel_id=1, source_target_pairs={{0,128},{16,144},{32,160},{48,176},{64,192},{80,208},{96,224},{112... | collective-permute-start | bytes 681992 | tf_op jit(solution)/shard_map/ppermute | solution.py:19
  98.5 0.9 collective-permute-done.4
  99.5 2.8 %collective-permute-done.9 = f32[37,12,128]{2,0,1:T(8,128)S(1)} collective-permute-done((f32[37,12,128]{2,0,1:T(8,128)S(1)}, f32[37,12,128]{2,0,1:T(8,128)S(1)}, u32[]{:S(2)}, u32[]{:S(2)}) %collective-permute-start.9) | collective-permute-done | bytes 227360 | tf_op jit(solution)/shard_map/ppermute | solution.py:19
  102.4 0.5 fusion.3
  102.9 0.2 multiply_add_fusion.1
  103.1 0.4 pad_maximum_fusion
  103.5 1.3 fusion
  104.8 36.0 %psum.22 = f32[5,256]{1,0:T(8,128)S(1)} all-reduce(f32[5,256]{1,0:T(8,128)S(1)} %fusion), channel_id=1, replica_groups=mesh['sec'=16,'vel'=16] {'vel'}, use_global_device_ids=true, to_apply=%region_1.0 | all-reduce | flops 1280 | bytes 10240 | tf_op jit(solution)/shard_map/psum | solution.py:205
  140.8 2.7 %collective-permute-start.14 = (f32[5,2,128]{2,1,0:T(2,128)S(1)}, f32[5,2,128]{2,1,0:T(2,128)S(1)}, u32[]{:S(2)}, u32[]{:S(2)}) collective-permute-start(f32[5,2,128]{2,1,0:T(2,128)S(1)} %reshape.259), channel_id=1, source_target_pairs={{0,32},{16,48},{32,64},{48,80},{64,96},{80,112},{96,128},{112,144}... | collective-permute-start | bytes 15368 | tf_op jit(solution)/shard_map/ppermute | solution.py:19
  143.6 1.3 collective-permute-start.15
  144.9 1.3 collective-permute-start.16
  146.2 1.3 collective-permute-start.17
  147.5 1.7 collective-permute-done.16
  149.2 2.9 %collective-permute-done.17 = f32[5,2,128]{2,1,0:T(2,128)S(1)} collective-permute-done((f32[5,2,128]{2,1,0:T(2,128)S(1)}, f32[5,2,128]{2,1,0:T(2,128)S(1)}, u32[]{:S(2)}, u32[]{:S(2)}) %collective-permute-start.17) | collective-permute-done | bytes 5152 | tf_op jit(solution)/shard_map/ppermute | solution.py:19
  152.8 1.9 abs_reduce_fusion
  154.8 0.7 subtract_reduce_fusion
  155.5 0.8 dynamic-slice_multiply_fusion
  156.3 0.1 reshape.263
  156.4 0.1 pad_maximum_fusion.10
  156.4 79.3 %psum.23 = f32[26]{0:T(128)S(1)} all-reduce(f32[26]{0:T(128)S(1)} %pad_maximum_fusion.10), channel_id=1, replica_groups=mesh['sec'=16,'vel'=16] {'sec','vel'}, use_global_device_ids=true, to_apply=%region_18.0 | all-reduce | flops 26 | bytes 208 | tf_op jit(solution)/shard_map/psum | solution.py:230
  235.8 0.7 fusion.36
  236.5 0.7 multiply_reduce_fusion.14
  244.7 0.7 multiply_reduce_fusion.13
  253.0 0.1 mul.489
  253.1 1.1 multiply_add_fusion
  (100 shorter events, 1.5 us)
Async XLA Ops:
  0.6 0.7 copy-start.4
  0.6 0.7 copy-start.6
  1.5 1.7 copy-start
  36.0 2.7 %copy-start.1 = (f32[25,256]{1,0:T(8,128)S(1)}, f32[25,256]{1,0:T(8,128)}, u32[]{:S(2)}) copy-start(f32[25,256]{1,0:T(8,128)} %param.13) | copy-start | bytes 76804
  36.0 2.7 %copy-start.2 = (f32[25,256]{1,0:T(8,128)S(1)}, f32[25,256]{1,0:T(8,128)}, u32[]{:S(2)}) copy-start(f32[25,256]{1,0:T(8,128)} %param.12) | copy-start | bytes 76804
  36.0 2.7 %copy-start.3 = (f32[25,256]{1,0:T(8,128)S(1)}, f32[25,256]{1,0:T(8,128)}, u32[]{:S(2)}) copy-start(f32[25,256]{1,0:T(8,128)} %param.11) | copy-start | bytes 76804
  36.0 30.5 %collective-permute-start = (f32[37,12,128]{2,0,1:T(8,128)S(1)}, f32[37,12,128]{2,0,1:T(8,128)S(1)}, u32[]{:S(2)}, u32[]{:S(2)}) collective-permute-start(f32[37,12,128]{2,0,1:T(8,128)S(1)} %pad_maximum_fusion.1), channel_id=1, source_target_pairs={{16,0},{32,16},{48,32},{64,48},{80,64},{96,80},{112,96},{128,112},... | collective-permute-start | bytes 681992 | tf_op jit(solution)/shard_map/ppermute | solution.py:19
  37.4 29.2 %collective-permute-start.1 = (f32[37,12,128]{2,0,1:T(8,128)S(1)}, f32[37,12,128]{2,0,1:T(8,128)S(1)}, u32[]{:S(2)}, u32[]{:S(2)}) collective-permute-start(f32[37,12,128]{2,0,1:T(8,128)S(1)} %pad_maximum_fusion.1), channel_id=1, source_target_pairs={{32,0},{48,16},{64,32},{80,48},{96,64},{112,80},{128,96},{144,112}... | collective-permute-start | bytes 681992 | tf_op jit(solution)/shard_map/ppermute | solution.py:19
  38.8 12.8 %collective-permute-start.10 = (f32[75,2,128]{2,1,0:T(2,128)S(1)}, f32[75,2,128]{2,1,0:T(2,128)S(1)}, u32[]{:S(2)}, u32[]{:S(2)}) collective-permute-start(f32[75,2,128]{2,1,0:T(2,128)S(1)} %reshape.257), channel_id=1, source_target_pairs={{0,32},{16,48},{32,64},{48,80},{64,96},{80,112},{96,128},{112,144}... | collective-permute-start | bytes 230408 | tf_op jit(solution)/shard_map/ppermute | solution.py:19
  45.0 7.9 %collective-permute-start.11 = (f32[75,2,128]{2,1,0:T(2,128)S(1)}, f32[75,2,128]{2,1,0:T(2,128)S(1)}, u32[]{:S(2)}, u32[]{:S(2)}) collective-permute-start(f32[75,2,128]{2,1,0:T(2,128)S(1)} %reshape.257), channel_id=1, source_target_pairs={{0,16},{16,32},{32,48},{48,64},{64,80},{80,96},{96,112},{112,128},... | collective-permute-start | bytes 230408 | tf_op jit(solution)/shard_map/ppermute | solution.py:19
  48.3 9.4 %collective-permute-start.12 = (f32[75,2,128]{2,1,0:T(2,128)S(1)}, f32[75,2,128]{2,1,0:T(2,128)S(1)}, u32[]{:S(2)}, u32[]{:S(2)}) collective-permute-start(f32[75,2,128]{2,1,0:T(2,128)S(1)} %reshape.257), channel_id=1, source_target_pairs={{16,0},{32,16},{48,32},{64,48},{80,64},{96,80},{112,96},{128,112},... | collective-permute-start | bytes 230408 | tf_op jit(solution)/shard_map/ppermute | solution.py:19
  51.6 12.9 %collective-permute-start.13 = (f32[75,2,128]{2,1,0:T(2,128)S(1)}, f32[75,2,128]{2,1,0:T(2,128)S(1)}, u32[]{:S(2)}, u32[]{:S(2)}) collective-permute-start(f32[75,2,128]{2,1,0:T(2,128)S(1)} %reshape.257), channel_id=1, source_target_pairs={{32,0},{48,16},{64,32},{80,48},{96,64},{112,80},{128,96},{144,112}... | collective-permute-start | bytes 230408 | tf_op jit(solution)/shard_map/ppermute | solution.py:19
  52.9 15.1 %collective-permute-start.5 = (f32[37,12,128]{2,0,1:T(8,128)S(1)}, f32[37,12,128]{2,0,1:T(8,128)S(1)}, u32[]{:S(2)}, u32[]{:S(2)}) collective-permute-start(f32[37,12,128]{2,0,1:T(8,128)S(1)} %pad_maximum_fusion.5), channel_id=1, source_target_pairs={{0,16},{16,32},{32,48},{48,64},{64,80},{80,96},{96,112},{112,128},... | collective-permute-start | bytes 681992 | tf_op jit(solution)/shard_map/ppermute | solution.py:19
  57.6 11.1 %collective-permute-start.6 = (f32[37,12,128]{2,0,1:T(8,128)S(1)}, f32[37,12,128]{2,0,1:T(8,128)S(1)}, u32[]{:S(2)}, u32[]{:S(2)}) collective-permute-start(f32[37,12,128]{2,0,1:T(8,128)S(1)} %pad_maximum_fusion.5), channel_id=1, source_target_pairs={{0,32},{16,48},{32,64},{48,80},{64,96},{80,112},{96,128},{112,144}... | collective-permute-start | bytes 681992 | tf_op jit(solution)/shard_map/ppermute | solution.py:19
  66.7 8.7 %collective-permute-start.2 = (f32[37,12,128]{2,0,1:T(8,128)S(1)}, f32[37,12,128]{2,0,1:T(8,128)S(1)}, u32[]{:S(2)}, u32[]{:S(2)}) collective-permute-start(f32[37,12,128]{2,0,1:T(8,128)S(1)} %pad_maximum_fusion.2), channel_id=1, source_target_pairs={{32,0},{48,16},{64,32},{80,48},{96,64},{112,80},{128,96},{144,112}... | collective-permute-start | bytes 681992 | tf_op jit(solution)/shard_map/ppermute | solution.py:19
  68.8 12.3 %collective-permute-start.7 = (f32[37,12,128]{2,0,1:T(8,128)S(1)}, f32[37,12,128]{2,0,1:T(8,128)S(1)}, u32[]{:S(2)}, u32[]{:S(2)}) collective-permute-start(f32[37,12,128]{2,0,1:T(8,128)S(1)} %pad_maximum_fusion.6), channel_id=1, source_target_pairs={{0,32},{16,48},{32,64},{48,80},{64,96},{80,112},{96,128},{112,144}... | collective-permute-start | bytes 681992 | tf_op jit(solution)/shard_map/ppermute | solution.py:19
  75.5 15.4 %collective-permute-start.3 = (f32[37,12,128]{2,0,1:T(8,128)S(1)}, f32[37,12,128]{2,0,1:T(8,128)S(1)}, u32[]{:S(2)}, u32[]{:S(2)}) collective-permute-start(f32[37,12,128]{2,0,1:T(8,128)S(1)} %pad_maximum_fusion.3), channel_id=1, source_target_pairs={{64,0},{80,16},{96,32},{112,48},{128,64},{144,80},{160,96},{176,11... | collective-permute-start | bytes 681992 | tf_op jit(solution)/shard_map/ppermute | solution.py:19
  81.3 11.2 %collective-permute-start.8 = (f32[37,12,128]{2,0,1:T(8,128)S(1)}, f32[37,12,128]{2,0,1:T(8,128)S(1)}, u32[]{:S(2)}, u32[]{:S(2)}) collective-permute-start(f32[37,12,128]{2,0,1:T(8,128)S(1)} %pad_maximum_fusion.7), channel_id=1, source_target_pairs={{0,64},{16,80},{32,96},{48,112},{64,128},{80,144},{96,160},{112,17... | collective-permute-start | bytes 681992 | tf_op jit(solution)/shard_map/ppermute | solution.py:19
  91.0 8.4 %collective-permute-start.4 = (f32[37,12,128]{2,0,1:T(8,128)S(1)}, f32[37,12,128]{2,0,1:T(8,128)S(1)}, u32[]{:S(2)}, u32[]{:S(2)}) collective-permute-start(f32[37,12,128]{2,0,1:T(8,128)S(1)} %pad_maximum_fusion.4), channel_id=1, source_target_pairs={{128,0},{144,16},{160,32},{176,48},{192,64},{208,80},{224,96},{240... | collective-permute-start | bytes 681992 | tf_op jit(solution)/shard_map/ppermute | solution.py:19
  92.6 9.7 %collective-permute-start.9 = (f32[37,12,128]{2,0,1:T(8,128)S(1)}, f32[37,12,128]{2,0,1:T(8,128)S(1)}, u32[]{:S(2)}, u32[]{:S(2)}) collective-permute-start(f32[37,12,128]{2,0,1:T(8,128)S(1)} %pad_maximum_fusion.8), channel_id=1, source_target_pairs={{0,128},{16,144},{32,160},{48,176},{64,192},{80,208},{96,224},{112... | collective-permute-start | bytes 681992 | tf_op jit(solution)/shard_map/ppermute | solution.py:19
  140.8 6.7 %collective-permute-start.14 = (f32[5,2,128]{2,1,0:T(2,128)S(1)}, f32[5,2,128]{2,1,0:T(2,128)S(1)}, u32[]{:S(2)}, u32[]{:S(2)}) collective-permute-start(f32[5,2,128]{2,1,0:T(2,128)S(1)} %reshape.259), channel_id=1, source_target_pairs={{0,32},{16,48},{32,64},{48,80},{64,96},{80,112},{96,128},{112,144}... | collective-permute-start | bytes 15368 | tf_op jit(solution)/shard_map/ppermute | solution.py:19
  143.6 4.0 %collective-permute-start.15 = (f32[5,2,128]{2,1,0:T(2,128)S(1)}, f32[5,2,128]{2,1,0:T(2,128)S(1)}, u32[]{:S(2)}, u32[]{:S(2)}) collective-permute-start(f32[5,2,128]{2,1,0:T(2,128)S(1)} %reshape.259), channel_id=1, source_target_pairs={{0,16},{16,32},{32,48},{48,64},{64,80},{80,96},{96,112},{112,128},... | collective-permute-start | bytes 15368 | tf_op jit(solution)/shard_map/ppermute | solution.py:19
  144.9 4.4 %collective-permute-start.16 = (f32[5,2,128]{2,1,0:T(2,128)S(1)}, f32[5,2,128]{2,1,0:T(2,128)S(1)}, u32[]{:S(2)}, u32[]{:S(2)}) collective-permute-start(f32[5,2,128]{2,1,0:T(2,128)S(1)} %reshape.259), channel_id=1, source_target_pairs={{16,0},{32,16},{48,32},{64,48},{80,64},{96,80},{112,96},{128,112},... | collective-permute-start | bytes 15368 | tf_op jit(solution)/shard_map/ppermute | solution.py:19
  146.2 6.0 %collective-permute-start.17 = (f32[5,2,128]{2,1,0:T(2,128)S(1)}, f32[5,2,128]{2,1,0:T(2,128)S(1)}, u32[]{:S(2)}, u32[]{:S(2)}) collective-permute-start(f32[5,2,128]{2,1,0:T(2,128)S(1)} %reshape.259), channel_id=1, source_target_pairs={{32,0},{48,16},{64,32},{80,48},{96,64},{112,80},{128,96},{144,112}... | collective-permute-start | bytes 15368 | tf_op jit(solution)/shard_map/ppermute | solution.py:19
  235.8 0.7 copy-start.5
  235.8 0.7 copy-start.7
where the time goes:
time: 255 us; the launch traced here: 254 us
  blocking collectives  143 us (56%)
  starting transfers between devices  56.1 us (22%)
  between operations  16.8 us (7%)
  waiting for transfers between devices  16.2 us (6%)
  other arithmetic  8.25 us (3%)
  local copies, waits for them, and re-layouts  7.31 us (3%)
  matrix products  6.31 us (2%)
    psum x1, blocking collectives, body(): lax.psum(jnp.concatenate([line_loaded, local_totals * first_copy]), ('sec...  79.3 us
    ppermute x18, starting transfers between devices, passed_along(): return lax.ppermute(block, axis, route)  56.1 us
    psum x1, blocking collectives, body(): lax.psum(jnp.dot(weighted, half_field, precision=HIGH), 'vel')  36 us
    psum x1, blocking collectives, body(): lax.psum(jnp.dot(weighted, distribution, precision=HIGH), 'vel')  27.9 us
    ppermute x18, waiting for transfers between devices, passed_along(): return lax.ppermute(block, axis, route)  16.2 us
  transfers between devices with their start and end apart: 18, of which 9 were waited for; matrix products, arithmetic and copies ran while one was open for 2% of the time, Pallas kernels for 0%

commit v1 on v0

--- a/solution.py
+++ b/solution.py
@@ -227,7 +227,9 @@
     magnitude = jnp.sum(jnp.abs(synthetic), axis=1)
     line_loaded = jnp.sum((node_mass * magnitude).reshape(node_rows, NXI), axis=0)
     first_copy = (lax.axis_index("vel") == 0).astype(jnp.float32)
-    gathered = lax.psum(jnp.concatenate([line_loaded, local_totals * first_copy]), ("sec", "vel"))
+    gathered = lax.psum(
+        lax.psum(jnp.concatenate([line_loaded, local_totals * first_copy]), "sec"), "vel"
+    )
     loaded = gathered[:NXI]
     goals = gathered[NXI:]
     shift_mass = jnp.zeros((), jnp.float32)

time: 255 us -> 239 us (0.937)
  blocking collectives: 143 us -> 127 us
    psum x1 -> x2, blocking collectives: 79.3 us -> 63 us  [the longest x1 31.8 us: body(): lax.psum(lax.psum(jnp.concatenate([line_loaded, local_totals * first_copy...]
where the time goes in v1:
time: 239 us; the launch traced here: 238 us
  blocking collectives  127 us (53%)
  starting transfers between devices  56.1 us (23%)
  between operations  16.8 us (7%)
  waiting for transfers between devices  16.2 us (7%)
  other arithmetic  8.25 us (3%)
  local copies, waits for them, and re-layouts  7.31 us (3%)
  matrix products  6.31 us (3%)
    ppermute x18, starting transfers between devices, passed_along(): return lax.ppermute(block, axis, route)  56.1 us
    psum x1, blocking collectives, body(): lax.psum(jnp.dot(weighted, half_field, precision=HIGH), 'vel')  36 us
    psum x1, blocking collectives, body(): lax.psum(lax.psum(jnp.concatenate([line_loaded, local_totals * first_copy...  31.8 us
    psum x1, blocking collectives, body(): lax.psum(jnp.concatenate([line_loaded, local_totals * first_copy]), 'sec')  31.2 us
    psum x1, blocking collectives, body(): lax.psum(jnp.dot(weighted, distribution, precision=HIGH), 'vel')  27.9 us
    ppermute x18, waiting for transfers between devices, passed_along(): return lax.ppermute(block, axis, route)  16.2 us
  transfers between devices with their start and end apart: 18, of which 9 were waited for; matrix products, arithmetic and copies ran while one was open for 2% of the time, Pallas kernels for 0%

profile of v1, /device:TPU:1, one launch (start us, length us, event | category | flops | bytes accessed | tf_op | source)
XLA Modules:
  0.0 237.8 jit_solution(10836248660838269395)
XLA Ops:
  0.6 0.0 copy-start.6
  0.7 0.7 copy-done.4
  1.3 0.1 add_add_fusion
  1.4 0.1 add_divide_fusion.1
  1.5 0.0 copy-start
  1.5 1.7 reshape.255
  3.2 1.3 fusion.13
  4.5 27.9 %psum.28 = f32[5,256]{1,0:T(8,128)S(1)} all-reduce(f32[5,256]{1,0:T(8,128)S(1)} %fusion.13), channel_id=1, replica_groups=mesh['sec'=16,'vel'=16] {'vel'}, use_global_device_ids=true, to_apply=%region_0.0 | all-reduce | flops 1280 | bytes 10240 | tf_op jit(solution)/shard_map/psum | solution.py:172
  32.4 1.8 fusion.16
  34.3 0.5 reshape.254
  34.8 0.1 add_divide_fusion
  34.9 0.7 fusion.29
  35.6 0.4 fusion.10
  36.0 0.0 copy-start.1
  36.0 1.3 collective-permute-start
  37.4 1.3 collective-permute-start.1
  38.8 6.2 %collective-permute-start.10 = (f32[75,2,128]{2,1,0:T(2,128)S(1)}, f32[75,2,128]{2,1,0:T(2,128)S(1)}, u32[]{:S(2)}, u32[]{:S(2)}) collective-permute-start(f32[75,2,128]{2,1,0:T(2,128)S(1)} %reshape.257), channel_id=1, source_target_pairs={{0,32},{16,48},{32,64},{48,80},{64,96},{80,112},{96,128},{112,144}... | collective-permute-start | bytes 230408 | tf_op jit(solution)/shard_map/ppermute | solution.py:19
  45.0 3.2 %collective-permute-start.11 = (f32[75,2,128]{2,1,0:T(2,128)S(1)}, f32[75,2,128]{2,1,0:T(2,128)S(1)}, u32[]{:S(2)}, u32[]{:S(2)}) collective-permute-start(f32[75,2,128]{2,1,0:T(2,128)S(1)} %reshape.257), channel_id=1, source_target_pairs={{0,16},{16,32},{32,48},{48,64},{64,80},{80,96},{96,112},{112,128},... | collective-permute-start | bytes 230408 | tf_op jit(solution)/shard_map/ppermute | solution.py:19
  48.3 1.3 collective-permute-start.12
  49.6 0.3 pad_add_fusion.1
  49.9 1.1 rev.8
  51.1 0.4 fusion.11
  51.6 1.3 collective-permute-start.13
  52.9 4.7 %collective-permute-start.5 = (f32[37,12,128]{2,0,1:T(8,128)S(1)}, f32[37,12,128]{2,0,1:T(8,128)S(1)}, u32[]{:S(2)}, u32[]{:S(2)}) collective-permute-start(f32[37,12,128]{2,0,1:T(8,128)S(1)} %pad_maximum_fusion.5), channel_id=1, source_target_pairs={{0,16},{16,32},{32,48},{48,64},{64,80},{80,96},{96,112},{112,128},... | collective-permute-start | bytes 681992 | tf_op jit(solution)/shard_map/ppermute | solution.py:19
  57.6 6.8 %collective-permute-start.6 = (f32[37,12,128]{2,0,1:T(8,128)S(1)}, f32[37,12,128]{2,0,1:T(8,128)S(1)}, u32[]{:S(2)}, u32[]{:S(2)}) collective-permute-start(f32[37,12,128]{2,0,1:T(8,128)S(1)} %pad_maximum_fusion.5), channel_id=1, source_target_pairs={{0,32},{16,48},{32,64},{48,80},{64,96},{80,112},{96,128},{112,144}... | collective-permute-start | bytes 681992 | tf_op jit(solution)/shard_map/ppermute | solution.py:19
  64.4 2.1 concatenate.91
  66.6 0.1 slice_add_fusion.1
  66.7 1.3 collective-permute-start.2
  68.0 0.7 collective-permute-done.6
  68.7 0.1 slice_add_fusion
  68.8 5.4 %collective-permute-start.7 = (f32[37,12,128]{2,0,1:T(8,128)S(1)}, f32[37,12,128]{2,0,1:T(8,128)S(1)}, u32[]{:S(2)}, u32[]{:S(2)}) collective-permute-start(f32[37,12,128]{2,0,1:T(8,128)S(1)} %pad_maximum_fusion.6), channel_id=1, source_target_pairs={{0,32},{16,48},{32,64},{48,80},{64,96},{80,112},{96,128},{112,144}... | collective-permute-start | bytes 681992 | tf_op jit(solution)/shard_map/ppermute | solution.py:19
  74.3 1.2 collective-permute-done.2
  75.5 1.3 collective-permute-start.3
  76.8 4.3 %collective-permute-done.7 = f32[37,12,128]{2,0,1:T(8,128)S(1)} collective-permute-done((f32[37,12,128]{2,0,1:T(8,128)S(1)}, f32[37,12,128]{2,0,1:T(8,128)S(1)}, u32[]{:S(2)}, u32[]{:S(2)}) %collective-permute-start.7) | collective-permute-done | bytes 227360 | tf_op jit(solution)/shard_map/ppermute | solution.py:19
  81.3 8.1 %collective-permute-start.8 = (f32[37,12,128]{2,0,1:T(8,128)S(1)}, f32[37,12,128]{2,0,1:T(8,128)S(1)}, u32[]{:S(2)}, u32[]{:S(2)}) collective-permute-start(f32[37,12,128]{2,0,1:T(8,128)S(1)} %pad_maximum_fusion.7), channel_id=1, source_target_pairs={{0,64},{16,80},{32,96},{48,112},{64,128},{80,144},{96,160},{112,17... | collective-permute-start | bytes 681992 | tf_op jit(solution)/shard_map/ppermute | solution.py:19
  89.4 1.5 collective-permute-done.3
  91.0 1.3 collective-permute-start.4
  92.3 0.2 collective-permute-done.8
  92.6 5.9 %collective-permute-start.9 = (f32[37,12,128]{2,0,1:T(8,128)S(1)}, f32[37,12,128]{2,0,1:T(8,128)S(1)}, u32[]{:S(2)}, u32[]{:S(2)}) collective-permute-start(f32[37,12,128]{2,0,1:T(8,128)S(1)} %pad_maximum_fusion.8), channel_id=1, source_target_pairs={{0,128},{16,144},{32,160},{48,176},{64,192},{80,208},{96,224},{112... | collective-permute-start | bytes 681992 | tf_op jit(solution)/shard_map/ppermute | solution.py:19
  98.5 0.9 collective-permute-done.4
  99.5 2.8 %collective-permute-done.9 = f32[37,12,128]{2,0,1:T(8,128)S(1)} collective-permute-done((f32[37,12,128]{2,0,1:T(8,128)S(1)}, f32[37,12,128]{2,0,1:T(8,128)S(1)}, u32[]{:S(2)}, u32[]{:S(2)}) %collective-permute-start.9) | collective-permute-done | bytes 227360 | tf_op jit(solution)/shard_map/ppermute | solution.py:19
  102.4 0.5 fusion.3
  102.9 0.2 multiply_add_fusion.1
  103.1 0.4 pad_maximum_fusion
  103.5 1.3 fusion
  104.8 36.0 %psum.29 = f32[5,256]{1,0:T(8,128)S(1)} all-reduce(f32[5,256]{1,0:T(8,128)S(1)} %fusion), channel_id=1, replica_groups=mesh['sec'=16,'vel'=16] {'vel'}, use_global_device_ids=true, to_apply=%region_1.0 | all-reduce | flops 1280 | bytes 10240 | tf_op jit(solution)/shard_map/psum | solution.py:205
  140.8 2.7 %collective-permute-start.14 = (f32[5,2,128]{2,1,0:T(2,128)S(1)}, f32[5,2,128]{2,1,0:T(2,128)S(1)}, u32[]{:S(2)}, u32[]{:S(2)}) collective-permute-start(f32[5,2,128]{2,1,0:T(2,128)S(1)} %reshape.259), channel_id=1, source_target_pairs={{0,32},{16,48},{32,64},{48,80},{64,96},{80,112},{96,128},{112,144}... | collective-permute-start | bytes 15368 | tf_op jit(solution)/shard_map/ppermute | solution.py:19
  143.6 1.3 collective-permute-start.15
  144.9 1.3 collective-permute-start.16
  146.2 1.3 collective-permute-start.17
  147.5 1.7 collective-permute-done.16
  149.2 2.9 %collective-permute-done.17 = f32[5,2,128]{2,1,0:T(2,128)S(1)} collective-permute-done((f32[5,2,128]{2,1,0:T(2,128)S(1)}, f32[5,2,128]{2,1,0:T(2,128)S(1)}, u32[]{:S(2)}, u32[]{:S(2)}) %collective-permute-start.17) | collective-permute-done | bytes 5152 | tf_op jit(solution)/shard_map/ppermute | solution.py:19
  152.8 1.9 abs_reduce_fusion
  154.8 0.7 subtract_reduce_fusion
  155.5 0.8 dynamic-slice_multiply_fusion
  156.3 0.1 reshape.263
  156.4 0.1 pad_maximum_fusion.10
  156.4 31.2 %psum.30 = f32[26]{0:T(128)S(1)} all-reduce(f32[26]{0:T(128)S(1)} %pad_maximum_fusion.10), channel_id=1, replica_groups=mesh['sec'=16,'vel'=16] {'sec'}, use_global_device_ids=true, to_apply=%region_18.0 | all-reduce | flops 26 | bytes 208 | tf_op jit(solution)/shard_map/psum | solution.py:231
  187.6 31.8 %psum.31 = f32[26]{0:T(128)S(1)} all-reduce(f32[26]{0:T(128)S(1)} %psum.30), channel_id=1, replica_groups=mesh['sec'=16,'vel'=16] {'vel'}, use_global_device_ids=true, to_apply=%region_19.0 | all-reduce | flops 26 | bytes 208 | tf_op jit(solution)/shard_map/psum | solution.py:230
  219.4 0.7 fusion.36
  220.1 0.7 multiply_reduce_fusion.14
  228.3 0.7 multiply_reduce_fusion.13
  236.6 0.1 mul.489
  236.7 1.1 multiply_add_fusion
  (101 shorter events, 1.5 us)
Async XLA Ops:
  0.6 0.7 copy-start.4
  0.6 0.7 copy-start.6
  1.5 1.7 copy-start
  36.0 2.7 %copy-start.1 = (f32[25,256]{1,0:T(8,128)S(1)}, f32[25,256]{1,0:T(8,128)}, u32[]{:S(2)}) copy-start(f32[25,256]{1,0:T(8,128)} %param.13) | copy-start | bytes 76804
  36.0 2.7 %copy-start.2 = (f32[25,256]{1,0:T(8,128)S(1)}, f32[25,256]{1,0:T(8,128)}, u32[]{:S(2)}) copy-start(f32[25,256]{1,0:T(8,128)} %param.12) | copy-start | bytes 76804
  36.0 2.7 %copy-start.3 = (f32[25,256]{1,0:T(8,128)S(1)}, f32[25,256]{1,0:T(8,128)}, u32[]{:S(2)}) copy-start(f32[25,256]{1,0:T(8,128)} %param.11) | copy-start | bytes 76804
  36.0 30.5 %collective-permute-start = (f32[37,12,128]{2,0,1:T(8,128)S(1)}, f32[37,12,128]{2,0,1:T(8,128)S(1)}, u32[]{:S(2)}, u32[]{:S(2)}) collective-permute-start(f32[37,12,128]{2,0,1:T(8,128)S(1)} %pad_maximum_fusion.1), channel_id=1, source_target_pairs={{16,0},{32,16},{48,32},{64,48},{80,64},{96,80},{112,96},{128,112},... | collective-permute-start | bytes 681992 | tf_op jit(solution)/shard_map/ppermute | solution.py:19
  37.4 29.2 %collective-permute-start.1 = (f32[37,12,128]{2,0,1:T(8,128)S(1)}, f32[37,12,128]{2,0,1:T(8,128)S(1)}, u32[]{:S(2)}, u32[]{:S(2)}) collective-permute-start(f32[37,12,128]{2,0,1:T(8,128)S(1)} %pad_maximum_fusion.1), channel_id=1, source_target_pairs={{32,0},{48,16},{64,32},{80,48},{96,64},{112,80},{128,96},{144,112}... | collective-permute-start | bytes 681992 | tf_op jit(solution)/shard_map/ppermute | solution.py:19
  38.8 12.8 %collective-permute-start.10 = (f32[75,2,128]{2,1,0:T(2,128)S(1)}, f32[75,2,128]{2,1,0:T(2,128)S(1)}, u32[]{:S(2)}, u32[]{:S(2)}) collective-permute-start(f32[75,2,128]{2,1,0:T(2,128)S(1)} %reshape.257), channel_id=1, source_target_pairs={{0,32},{16,48},{32,64},{48,80},{64,96},{80,112},{96,128},{112,144}... | collective-permute-start | bytes 230408 | tf_op jit(solution)/shard_map/ppermute | solution.py:19
  45.0 7.9 %collective-permute-start.11 = (f32[75,2,128]{2,1,0:T(2,128)S(1)}, f32[75,2,128]{2,1,0:T(2,128)S(1)}, u32[]{:S(2)}, u32[]{:S(2)}) collective-permute-start(f32[75,2,128]{2,1,0:T(2,128)S(1)} %reshape.257), channel_id=1, source_target_pairs={{0,16},{16,32},{32,48},{48,64},{64,80},{80,96},{96,112},{112,128},... | collective-permute-start | bytes 230408 | tf_op jit(solution)/shard_map/ppermute | solution.py:19
  48.3 9.4 %collective-permute-start.12 = (f32[75,2,128]{2,1,0:T(2,128)S(1)}, f32[75,2,128]{2,1,0:T(2,128)S(1)}, u32[]{:S(2)}, u32[]{:S(2)}) collective-permute-start(f32[75,2,128]{2,1,0:T(2,128)S(1)} %reshape.257), channel_id=1, source_target_pairs={{16,0},{32,16},{48,32},{64,48},{80,64},{96,80},{112,96},{128,112},... | collective-permute-start | bytes 230408 | tf_op jit(solution)/shard_map/ppermute | solution.py:19
  51.6 12.9 %collective-permute-start.13 = (f32[75,2,128]{2,1,0:T(2,128)S(1)}, f32[75,2,128]{2,1,0:T(2,128)S(1)}, u32[]{:S(2)}, u32[]{:S(2)}) collective-permute-start(f32[75,2,128]{2,1,0:T(2,128)S(1)} %reshape.257), channel_id=1, source_target_pairs={{32,0},{48,16},{64,32},{80,48},{96,64},{112,80},{128,96},{144,112}... | collective-permute-start | bytes 230408 | tf_op jit(solution)/shard_map/ppermute | solution.py:19
  52.9 15.1 %collective-permute-start.5 = (f32[37,12,128]{2,0,1:T(8,128)S(1)}, f32[37,12,128]{2,0,1:T(8,128)S(1)}, u32[]{:S(2)}, u32[]{:S(2)}) collective-permute-start(f32[37,12,128]{2,0,1:T(8,128)S(1)} %pad_maximum_fusion.5), channel_id=1, source_target_pairs={{0,16},{16,32},{32,48},{48,64},{64,80},{80,96},{96,112},{112,128},... | collective-permute-start | bytes 681992 | tf_op jit(solution)/shard_map/ppermute | solution.py:19
  57.6 11.1 %collective-permute-start.6 = (f32[37,12,128]{2,0,1:T(8,128)S(1)}, f32[37,12,128]{2,0,1:T(8,128)S(1)}, u32[]{:S(2)}, u32[]{:S(2)}) collective-permute-start(f32[37,12,128]{2,0,1:T(8,128)S(1)} %pad_maximum_fusion.5), channel_id=1, source_target_pairs={{0,32},{16,48},{32,64},{48,80},{64,96},{80,112},{96,128},{112,144}... | collective-permute-start | bytes 681992 | tf_op jit(solution)/shard_map/ppermute | solution.py:19
  66.7 8.7 %collective-permute-start.2 = (f32[37,12,128]{2,0,1:T(8,128)S(1)}, f32[37,12,128]{2,0,1:T(8,128)S(1)}, u32[]{:S(2)}, u32[]{:S(2)}) collective-permute-start(f32[37,12,128]{2,0,1:T(8,128)S(1)} %pad_maximum_fusion.2), channel_id=1, source_target_pairs={{32,0},{48,16},{64,32},{80,48},{96,64},{112,80},{128,96},{144,112}... | collective-permute-start | bytes 681992 | tf_op jit(solution)/shard_map/ppermute | solution.py:19
  68.8 12.3 %collective-permute-start.7 = (f32[37,12,128]{2,0,1:T(8,128)S(1)}, f32[37,12,128]{2,0,1:T(8,128)S(1)}, u32[]{:S(2)}, u32[]{:S(2)}) collective-permute-start(f32[37,12,128]{2,0,1:T(8,128)S(1)} %pad_maximum_fusion.6), channel_id=1, source_target_pairs={{0,32},{16,48},{32,64},{48,80},{64,96},{80,112},{96,128},{112,144}... | collective-permute-start | bytes 681992 | tf_op jit(solution)/shard_map/ppermute | solution.py:19
  75.5 15.4 %collective-permute-start.3 = (f32[37,12,128]{2,0,1:T(8,128)S(1)}, f32[37,12,128]{2,0,1:T(8,128)S(1)}, u32[]{:S(2)}, u32[]{:S(2)}) collective-permute-start(f32[37,12,128]{2,0,1:T(8,128)S(1)} %pad_maximum_fusion.3), channel_id=1, source_target_pairs={{64,0},{80,16},{96,32},{112,48},{128,64},{144,80},{160,96},{176,11... | collective-permute-start | bytes 681992 | tf_op jit(solution)/shard_map/ppermute | solution.py:19
  81.3 11.2 %collective-permute-start.8 = (f32[37,12,128]{2,0,1:T(8,128)S(1)}, f32[37,12,128]{2,0,1:T(8,128)S(1)}, u32[]{:S(2)}, u32[]{:S(2)}) collective-permute-start(f32[37,12,128]{2,0,1:T(8,128)S(1)} %pad_maximum_fusion.7), channel_id=1, source_target_pairs={{0,64},{16,80},{32,96},{48,112},{64,128},{80,144},{96,160},{112,17... | collective-permute-start | bytes 681992 | tf_op jit(solution)/shard_map/ppermute | solution.py:19
  91.0 8.4 %collective-permute-start.4 = (f32[37,12,128]{2,0,1:T(8,128)S(1)}, f32[37,12,128]{2,0,1:T(8,128)S(1)}, u32[]{:S(2)}, u32[]{:S(2)}) collective-permute-start(f32[37,12,128]{2,0,1:T(8,128)S(1)} %pad_maximum_fusion.4), channel_id=1, source_target_pairs={{128,0},{144,16},{160,32},{176,48},{192,64},{208,80},{224,96},{240... | collective-permute-start | bytes 681992 | tf_op jit(solution)/shard_map/ppermute | solution.py:19
  92.6 9.7 %collective-permute-start.9 = (f32[37,12,128]{2,0,1:T(8,128)S(1)}, f32[37,12,128]{2,0,1:T(8,128)S(1)}, u32[]{:S(2)}, u32[]{:S(2)}) collective-permute-start(f32[37,12,128]{2,0,1:T(8,128)S(1)} %pad_maximum_fusion.8), channel_id=1, source_target_pairs={{0,128},{16,144},{32,160},{48,176},{64,192},{80,208},{96,224},{112... | collective-permute-start | bytes 681992 | tf_op jit(solution)/shard_map/ppermute | solution.py:19
  140.8 6.7 %collective-permute-start.14 = (f32[5,2,128]{2,1,0:T(2,128)S(1)}, f32[5,2,128]{2,1,0:T(2,128)S(1)}, u32[]{:S(2)}, u32[]{:S(2)}) collective-permute-start(f32[5,2,128]{2,1,0:T(2,128)S(1)} %reshape.259), channel_id=1, source_target_pairs={{0,32},{16,48},{32,64},{48,80},{64,96},{80,112},{96,128},{112,144}... | collective-permute-start | bytes 15368 | tf_op jit(solution)/shard_map/ppermute | solution.py:19
  143.6 4.0 %collective-permute-start.15 = (f32[5,2,128]{2,1,0:T(2,128)S(1)}, f32[5,2,128]{2,1,0:T(2,128)S(1)}, u32[]{:S(2)}, u32[]{:S(2)}) collective-permute-start(f32[5,2,128]{2,1,0:T(2,128)S(1)} %reshape.259), channel_id=1, source_target_pairs={{0,16},{16,32},{32,48},{48,64},{64,80},{80,96},{96,112},{112,128},... | collective-permute-start | bytes 15368 | tf_op jit(solution)/shard_map/ppermute | solution.py:19
  144.9 4.4 %collective-permute-start.16 = (f32[5,2,128]{2,1,0:T(2,128)S(1)}, f32[5,2,128]{2,1,0:T(2,128)S(1)}, u32[]{:S(2)}, u32[]{:S(2)}) collective-permute-start(f32[5,2,128]{2,1,0:T(2,128)S(1)} %reshape.259), channel_id=1, source_target_pairs={{16,0},{32,16},{48,32},{64,48},{80,64},{96,80},{112,96},{128,112},... | collective-permute-start | bytes 15368 | tf_op jit(solution)/shard_map/ppermute | solution.py:19
  146.2 6.0 %collective-permute-start.17 = (f32[5,2,128]{2,1,0:T(2,128)S(1)}, f32[5,2,128]{2,1,0:T(2,128)S(1)}, u32[]{:S(2)}, u32[]{:S(2)}) collective-permute-start(f32[5,2,128]{2,1,0:T(2,128)S(1)} %reshape.259), channel_id=1, source_target_pairs={{32,0},{48,16},{64,32},{80,48},{96,64},{112,80},{128,96},{144,112}... | collective-permute-start | bytes 15368 | tf_op jit(solution)/shard_map/ppermute | solution.py:19
  219.4 0.7 copy-start.5
  219.4 0.7 copy-start.7
